TPU v7x, 128 devices: a whole 4x4x4 slice. The times are simulated.
128 devices in a mesh: grp: 4 (over z), dev: 32 (over x, y, core).
Axes of the slice: x: 4, y: 4, z: 4, core: 2. Of those that a mesh axis runs over, the one named last changes fastest.
Arguments:
- packed_w: bfloat16 [4, 8192, 8192], P(None, 'dev', 'grp'), may hold values from -0.0625 to 0.0625
- packed_t: bfloat16 [4, 8192, 1536], P(None, 'dev', 'grp'), may hold values from -6 to 6
- row_energy: float32 [4, 8192], P('grp', 'dev'), may hold values from 0.3 to 4
- col_energy: float32 [4, 1536], P('grp'), may hold values from 0.3 to 4
- block_order: int32 [4], replicated, may hold values from 3072 to 8192, as said below
Outputs:
- new_amps: float32 [4, 8192, 1536], P(None, 'dev', 'grp')
Inputs may be any that keep to these rules, and one draw needn't show every extreme that they name: `block_order`: one block has order exactly 8192; the others lie between 3072 and 8191.
All inputs are finite; a program needn't handle non-finite values.
Results may differ from a plain program's by a relative error of at most 0.0003.
Values may be sent and summed in bfloat16 or wider, within the bound.
No kernel may reach another device: no remote copies, remote signals or barrier semaphores. Data moves between devices by JAX's collectives and lax.ppermute only.
A program may use at most 192 MiB of HBM per device.

v0:
```python
import jax
import jax.numpy as jnp
from jax import lax
from jax.sharding import Mesh, NamedSharding, PartitionSpec as P


def apply_update(t_rows, cycle, live, row_gap, col_gap):
    denom = row_gap[:, None] + col_gap[None, :]
    update = jnp.where(live[:, None], cycle / denom, jnp.zeros_like(cycle))
    return t_rows.astype(jnp.float32) + update


def shards(packed_w, packed_t, row_energy, col_energy, block_order):
    nchip = lax.axis_size("chip")
    ncore = lax.axis_size("dc")
    rank = lax.axis_index("chip") * ncore + lax.axis_index("dc")
    group = lax.axis_index("grp")
    local = packed_t.shape[1]
    ndev = nchip * ncore
    true_rows = jnp.arange(local, dtype=jnp.int32) * ndev + rank
    t_rows = lax.all_to_all(packed_t, "grp", split_axis=0, concat_axis=2, tiled=True)[0]
    order = lax.dynamic_index_in_dim(block_order, group, 0, keepdims=False)
    live = true_rows < order
    t_live = jnp.where(live[:, None], t_rows, jnp.zeros_like(t_rows))
    t_half = lax.all_gather(t_live, "chip", axis=0, tiled=True)
    w_rows = lax.all_to_all(packed_w, "grp", split_axis=0, concat_axis=2, tiled=True)[0]
    w4 = w_rows.reshape(local, nchip, ncore, local)
    w_mine = lax.all_to_all(w4, "dc", split_axis=2, concat_axis=0, tiled=True)
    w_mine = w_mine.reshape(ncore * local, nchip * local)
    partial = jnp.dot(w_mine, t_half, preferred_element_type=jnp.float32)
    cycle = lax.psum_scatter(partial, "dc", scatter_dimension=0, tiled=True)
    new_block = apply_update(t_rows, cycle, live, row_energy[0], col_energy[0])
    return lax.all_to_all(new_block[None], "grp", split_axis=2, concat_axis=0, tiled=True)


def solution(mesh):
    ngrp, ndev = mesh.devices.shape
    ncore = 2
    split = Mesh(mesh.devices.reshape(ngrp, ndev // ncore, ncore), ("grp", "chip", "dc"))
    rows = ("chip", "dc")
    in_specs = (P(None, rows, "grp"), P(None, rows, "grp"), P("grp", rows), P("grp", None), P())
    out_specs = P(None, rows, "grp")
    body = jax.shard_map(
        shards, mesh=split, in_specs=in_specs, out_specs=out_specs, check_vma=False
    )
    target = NamedSharding(mesh, P(None, "dev", "grp"))

    def run(*args):
        return lax.with_sharding_constraint(body(*args), target)

    return run
```

profile of v0, /device:TPU:0, one launch (start us, length us, event | category | flops | bytes accessed | tf_op | source)
XLA Modules:
  0.0 192.1 jit_solution(3250268429148516764)
XLA Ops:
  6.5 5.4 %all-to-all-start = ((bf16[4,256,384]{2,1,0:T(8,128)(2,1)}), bf16[4,256,384]{2,1,0:T(8,128)(2,1)S(1)}, u32[]{:S(2)}, u32[]{:S(2)}) async-start(bf16[4,256,384]{2,1,0:T(8,128)(2,1)} %param.6), calls=%async_computation | async-start | bytes 1572864 | tf_op jit(solution)/shard_map/all_to_all | solution.py:21
  12.0 0.0 all-gather.2.cloned.1.call-start
  12.0 1.2 dynamic_slice.4
  13.2 0.7 add_compare_fusion
  13.8 10.4 %all-to-all-done = bf16[4,256,384]{2,1,0:T(8,128)(2,1)S(1)} async-done(((bf16[4,256,384]{2,1,0:T(8,128)(2,1)}), bf16[4,256,384]{2,1,0:T(8,128)(2,1)S(1)}, u32[]{:S(2)}, u32[]{:S(2)}) %all-to-all-start) | async-done | bytes 786464 | tf_op jit(solution)/shard_map/all_to_all | solution.py:21
  24.2 0.3 copy.12
  24.5 1.0 bitcast_select_fusion
  25.5 0.0 all-gather.2.cloned.1.call-update
  25.5 0.0 reduce-scatter.2.cloned.1.call-start
  25.6 6.2 %copy.13 = bf16[4,256,2048]{1,2,0:T(8,128)(2,1)} copy(bf16[4,256,2048]{2,1,0:T(8,128)(2,1)} %param.5) | data formatting | bytes 8388608 | tf_op args[0]
  31.8 51.7 %all_to_all.63 = bf16[4,256,2048]{1,2,0:T(8,128)(2,1)S(1)} all-to-all(bf16[4,256,2048]{1,2,0:T(8,128)(2,1)} %copy.13), channel_id=1, replica_groups=mesh['grp'=4,'chip'=16,'dc'=2] {'grp'}, dimensions={0} | all-to-all | bytes 8388608 | tf_op jit(solution)/shard_map/all_to_all | solution.py:26
  83.5 0.4 copy.14
  83.9 8.2 %all_to_all.64 = bf16[256,16,2,256]{0,3,1,2:T(8,128)(2,1)} all-to-all(bf16[256,16,2,256]{0,3,1,2:T(8,128)(2,1)S(1)} %copy.14), channel_id=1, replica_groups=mesh['grp'=4,'chip'=16,'dc'=2] {'dc'}, dimensions={2} | all-to-all | bytes 8388608 | tf_op jit(solution)/shard_map/all_to_all | solution.py:28
  92.1 7.9 %copy.15 = bf16[2,256,16,1,256]{4,2,1,0,3:T(8,128)(2,1)} copy(bf16[2,256,16,1,256]{1,4,2,0,3:T(8,128)(2,1)} %bitcast.31) | data formatting | bytes 8388608 | tf_op jit(solution)/shard_map/all_to_all | solution.py:28
  100.0 6.3 %copy.18 = bf16[64,8,16,256]{3,1,2,0:T(8,128)(2,1)} copy(bf16[64,8,16,256]{3,2,1,0:T(8,128)(2,1)} %bitcast.32) | data formatting | bytes 8388608
  106.4 17.2 %all-gather.2.cloned.1.call-done = bf16[4096,1536]{0,1:T(8,128)(2,1)} async-done(((bf16[256,1536]{0,1:T(8,128)(2,1)}), bf16[4096,1536]{0,1:T(8,128)(2,1)}) %all-gather.2.cloned.1.call-update) | async-done | bytes 12582928 | tf_op jit(solution)/shard_map/all_gather | solution.py:25
  123.5 12.1 %convolution_bitcast_fusion = f32[512,1536]{0,1:T(8,128)} fusion(bf16[4096,1536]{0,1:T(8,128)(2,1)} %all-gather.2.cloned.1.call-done, bf16[512,4096]{1,0:T(8,128)(2,1)} %bitcast.34), kind=kOutput, calls=%fused_computation | convolution fusion | flops 6442450944 | bytes 19922944 | tf_op jit(solution)/shard_map/dot_general | solution.py:30
  135.6 0.0 copy-start
  135.6 0.0 copy-start.1
  135.6 0.0 reduce-scatter.2.cloned.1.call-update
  135.6 0.7 copy-done
  136.3 12.6 %reduce-scatter.2.cloned.1.call-done = f32[256,1536]{0,1:T(8,128)} async-done(((f32[512,1536]{0,1:T(8,128)}), f32[256,1536]{0,1:T(8,128)}) %reduce-scatter.2.cloned.1.call-update) | async-done | bytes 1572880 | tf_op jit(solution)/shard_map/reduce_scatter | solution.py:31
  148.9 0.0 copy-done.1
  148.9 1.8 add_bitcast_fusion
  150.7 6.5 %copy.16 = f32[1,256,1536]{1,0,2:T(1,128)S(1)} copy(f32[1,256,1536]{1,2,0:T(8,128)S(1)} %add_bitcast_fusion) | data formatting | bytes 3145728 | tf_op jit(solution)/shard_map/broadcast_in_dim | solution.py:33
  157.2 25.3 %all_to_all.65 = f32[1,256,1536]{1,0,2:T(1,128)S(1)} all-to-all(f32[1,256,1536]{1,0,2:T(1,128)S(1)} %copy.16), channel_id=1, replica_groups=mesh['grp'=4,'chip'=16,'dc'=2] {'grp'}, dimensions={2} | all-to-all | bytes 3145728 | tf_op jit(solution)/shard_map/all_to_all | solution.py:33
  182.5 2.7 %copy.17 = f32[1,256,4,384]{3,1,2,0:T(8,128)} copy(f32[1,256,4,384]{1,0,3,2:T(1,128)S(1)} %bitcast.33) | data formatting | bytes 3145728 | tf_op jit(solution)/shard_map/all_to_all | solution.py:33
  (1 shorter events, 0.0 us)
Async XLA Ops:
  6.5 17.7 %all-to-all-start = ((bf16[4,256,384]{2,1,0:T(8,128)(2,1)}), bf16[4,256,384]{2,1,0:T(8,128)(2,1)S(1)}, u32[]{:S(2)}, u32[]{:S(2)}) async-start(bf16[4,256,384]{2,1,0:T(8,128)(2,1)} %param.6), calls=%async_computation | async-start | bytes 1572864 | tf_op jit(solution)/shard_map/all_to_all | solution.py:21
  12.0 111.6 %all-gather.2.cloned.1.call-start = ((), (), s32[]{:S(2)}) async-start(), calls=%async_computation.5 | async-start | bytes 13369344 | tf_op jit(solution)/shard_map/all_gather | solution.py:25
  25.5 123.4 %reduce-scatter.2.cloned.1.call-start = ((), (), s32[]{:S(2)}) async-start(), calls=%async_computation.6 | async-start | bytes 4718592 | tf_op jit(solution)/shard_map/reduce_scatter | solution.py:31
  135.6 0.7 copy-start
  135.6 13.3 %copy-start.1 = (f32[1,256]{1,0:T(1,128)S(1)}, f32[1,256]{1,0:T(1,128)}, u32[]{:S(2)}) copy-start(f32[1,256]{1,0:T(1,128)} %param.7) | copy-start | bytes 3076
Sparse Core Ops, SparseCore 0:
  25.7 97.8 all-gather.1
  135.7 13.1 reduce-scatter.1
where the time goes:
time: 193 us; the launch traced here: 192 us
  blocking collectives  85.2 us (44%)
  waiting for transfers between devices  40.2 us (21%)
  local copies, waits for them, and re-layouts  32.3 us (17%)
  between operations  13.4 us (7%)
  matrix products  12.1 us (6%)
  starting transfers between devices  5.46 us (3%)
  other arithmetic  3.45 us (2%)
    all_to_all x1, blocking collectives, shards(): lax.all_to_all(packed_w, 'grp', split_axis=0, concat_axis=2, tiled=True)[0]  51.7 us
    all_to_all x1, blocking collectives, shards(): lax.all_to_all(new_block[None], 'grp', split_axis=2, concat_axis=0, tiled...  25.3 us
    all_gather x1, waiting for transfers between devices, shards(): t_half = lax.all_gather(t_live, 'chip', axis=0, tiled=True)  17.2 us
    unnamed x6, local copies, waits for them, and re-layouts  13.2 us
    reduce_scatter x1, waiting for transfers between devices, shards(): cycle = lax.psum_scatter(partial, 'dc', scatter_dimension=0, tiled=True)  12.6 us
    dot_general x1, matrix products, shards(): partial = jnp.dot(w_mine, t_half, preferred_element_type=jnp.float32)  12.1 us
    all_to_all x1, waiting for transfers between devices, shards(): lax.all_to_all(packed_t, 'grp', split_axis=0, concat_axis=2, tiled=True)[0]  10.4 us
    all_to_all x1, blocking collectives, shards(): w_mine = lax.all_to_all(w4, 'dc', split_axis=2, concat_axis=0, tiled=True)  8.16 us
  transfers between devices with their start and end apart: 3, of which 3 were waited for; matrix products, arithmetic and copies ran while one was open for 12% of the time, Pallas kernels for 0%

commit v1 on v0

--- a/solution.py
+++ b/solution.py
@@ -22,7 +22,13 @@
     order = lax.dynamic_index_in_dim(block_order, group, 0, keepdims=False)
     live = true_rows < order
     t_live = jnp.where(live[:, None], t_rows, jnp.zeros_like(t_rows))
-    t_half = lax.all_gather(t_live, "chip", axis=0, tiled=True)
+    lanes = []
+    for _ in range(lax.psum(1, "chip")):
+        lanes.append(t_live)
+    t_half = jnp.concatenate(
+        lax.all_to_all(jnp.stack(lanes, axis=0), axis_name="chip", split_axis=0, concat_axis=0),
+        axis=0,
+    )
     w_rows = lax.all_to_all(packed_w, "grp", split_axis=0, concat_axis=2, tiled=True)[0]
     w4 = w_rows.reshape(local, nchip, ncore, local)
     w_mine = lax.all_to_all(w4, "dc", split_axis=2, concat_axis=0, tiled=True)

time: 193 us -> 391 us (2.03)
  waiting for transfers between devices: 40.2 us -> 272 us
  blocking collectives: 85.2 us -> 33.5 us
  starting transfers between devices: 5.46 us -> 17.4 us
  local copies, waits for them, and re-layouts: 32.3 us -> 39.8 us
    all_to_all x0 -> x2, waiting for transfers between devices: none -> 248 us  [the longest x1 202 us: shards(): lax.all_to_all(jnp.stack(lanes, axis=0), axis_name='chip', split_axis=0,...]
    all_to_all x1 -> x0, blocking collectives: 51.7 us -> none  [shards(): lax.all_to_all(packed_w, 'grp', split_axis=0, concat_axis=2, tiled=True)[0]]
    all_gather x1 -> x0, waiting for transfers between devices: 17.2 us -> none  [shards(): t_half = lax.all_gather(t_live, 'chip', axis=0, tiled=True)]
    all_to_all x0 -> x2, starting transfers between devices: none -> 11.9 us  [the longest x1 7.08 us: shards(): lax.all_to_all(jnp.stack(lanes, axis=0), axis_name='chip', split_axis=0,...]
    another operation x0 -> x1, local copies, waits for them, and re-layouts: none -> 5.69 us  [shards(): jnp.stack(lanes, axis=0)]
    reduce_scatter x1, waiting for transfers between devices: 12.6 us -> 18 us  [shards(): cycle = lax.psum_scatter(partial, 'dc', scatter_dimension=0, tiled=True)]
    all_to_all x1, waiting for transfers between devices: 10.4 us -> 6.03 us  [shards(): lax.all_to_all(packed_t, 'grp', split_axis=0, concat_axis=2, tiled=True)[0]]
    unnamed x6 -> x8, local copies, waits for them, and re-layouts: 13.2 us -> 13.3 us
  transfers between devices with their start and end apart: 3 -> 4, of which waited for: 3 -> 4; matrix products, arithmetic and copies ran while one was open for 12% -> 6% of each run, Pallas kernels for 0% -> 0%
where the time goes in v1:
time: 391 us
  waiting for transfers between devices  272 us (70%)
  local copies, waits for them, and re-layouts  39.8 us (10%)
  blocking collectives  33.5 us (9%)
  starting transfers between devices  17.4 us (4%)
  between operations  13.5 us (3%)
  matrix products  12.1 us (3%)
    all_to_all x1, waiting for transfers between devices, shards(): lax.all_to_all(jnp.stack(lanes, axis=0), axis_name='chip', split_axis=0,...  202 us
    all_to_all x1, waiting for transfers between devices, shards(): lax.all_to_all(packed_w, 'grp', split_axis=0, concat_axis=2, tiled=True)[0]  46.1 us
    all_to_all x1, blocking collectives, shards(): lax.all_to_all(new_block[None], 'grp', split_axis=2, concat_axis=0, tiled...  25.3 us
    reduce_scatter x1, waiting for transfers between devices, shards(): cycle = lax.psum_scatter(partial, 'dc', scatter_dimension=0, tiled=True)  18 us
    unnamed x8, local copies, waits for them, and re-layouts  13.3 us
    dot_general x1, matrix products, shards(): partial = jnp.dot(w_mine, t_half, preferred_element_type=jnp.float32)  12.1 us
    all_to_all x1, blocking collectives, shards(): w_mine = lax.all_to_all(w4, 'dc', split_axis=2, concat_axis=0, tiled=True)  8.18 us
    all_to_all x1, local copies, waits for them, and re-layouts, shards(): w_mine = lax.all_to_all(w4, 'dc', split_axis=2, concat_axis=0, tiled=True)  7.99 us
  transfers between devices with their start and end apart: 4, of which 4 were waited for; matrix products, arithmetic and copies ran while one was open for 6% of the time, Pallas kernels for 0%

profile of v1, /device:TPU:0, one launch (start us, length us, event | category | flops | bytes accessed | tf_op | source)
XLA Modules:
  0.0 390.6 jit_solution(894100575223617009)
XLA Ops:
  6.5 5.4 %all-to-all-start = ((bf16[4,256,384]{2,1,0:T(8,128)(2,1)}), bf16[4,256,384]{2,1,0:T(8,128)(2,1)S(1)}, u32[]{:S(2)}, u32[]{:S(2)}) async-start(bf16[4,256,384]{2,1,0:T(8,128)(2,1)} %param.6), calls=%async_computation | async-start | bytes 1572864 | tf_op jit(solution)/shard_map/all_to_all | solution.py:21
  12.0 6.3 %copy.16 = bf16[4,256,2048]{1,2,0:T(8,128)(2,1)} copy(bf16[4,256,2048]{2,1,0:T(8,128)(2,1)} %param.5) | data formatting | bytes 8388608 | tf_op args[0]
  18.2 0.0 copy-start.2
  18.2 6.0 %all-to-all-done = bf16[4,256,384]{2,1,0:T(8,128)(2,1)S(1)} async-done(((bf16[4,256,384]{2,1,0:T(8,128)(2,1)}), bf16[4,256,384]{2,1,0:T(8,128)(2,1)S(1)}, u32[]{:S(2)}, u32[]{:S(2)}) %all-to-all-start) | async-done | bytes 786464 | tf_op jit(solution)/shard_map/all_to_all | solution.py:21
  24.2 4.8 %all-to-all-start.2 = ((bf16[4,256,2048]{1,2,0:T(8,128)(2,1)}), bf16[4,256,2048]{1,2,0:T(8,128)(2,1)}, u32[]{:S(2)}, u32[]{:S(2)}) async-start(bf16[4,256,2048]{1,2,0:T(8,128)(2,1)} %copy.16), calls=%async_computation.2 | async-start | bytes 8388608 | tf_op jit(solution)/shard_map/all_to_all | solution.py:32
  29.1 0.0 copy-done.2
  29.1 0.6 dynamic_slice.4
  29.7 0.7 add_compare_fusion
  30.3 0.3 copy.14
  30.6 0.1 bitcast_select_fusion
  30.7 0.3 copy.15
  31.0 46.1 %all-to-all-done.2 = bf16[4,256,2048]{1,2,0:T(8,128)(2,1)} async-done(((bf16[4,256,2048]{1,2,0:T(8,128)(2,1)}), bf16[4,256,2048]{1,2,0:T(8,128)(2,1)}, u32[]{:S(2)}, u32[]{:S(2)}) %all-to-all-start.2) | async-done | bytes 4194336 | tf_op jit(solution)/shard_map/all_to_all | solution.py:32
  77.1 2.5 copy.17
  79.6 8.2 %all_to_all.68 = bf16[256,16,2,256]{0,3,1,2:T(8,128)(2,1)} all-to-all(bf16[256,16,2,256]{0,3,1,2:T(8,128)(2,1)S(1)} %copy.17), channel_id=1, replica_groups=mesh['grp'=4,'chip'=16,'dc'=2] {'dc'}, dimensions={2} | all-to-all | bytes 8388608 | tf_op jit(solution)/shard_map/all_to_all | solution.py:34
  87.7 5.7 %stack.2 = bf16[16,256,1536]{2,1,0:T(8,128)(2,1)} broadcast(bf16[256,1536]{1,0:T(8,128)(2,1)S(1)} %copy.15), dimensions={1,2} | broadcast | bytes 13369344 | tf_op jit(solution)/shard_map/stack | solution.py:29
  93.4 7.1 %all-to-all-start.1 = ((bf16[16,256,1536]{2,1,0:T(8,128)(2,1)}), bf16[16,256,1536]{2,1,0:T(8,128)(2,1)}, u32[]{:S(2)}, u32[]{:S(2)}) async-start(bf16[16,256,1536]{2,1,0:T(8,128)(2,1)} %stack.2), calls=%async_computation.1 | async-start | bytes 25165824 | tf_op jit(solution)/shard_map/all_to_all | solution.py:29
  100.5 0.0 reduce-scatter.2.cloned.1.call-start
  100.6 8.0 %copy.18 = bf16[2,256,16,1,256]{4,2,1,0,3:T(8,128)(2,1)} copy(bf16[2,256,16,1,256]{1,4,2,0,3:T(8,128)(2,1)} %bitcast.31) | data formatting | bytes 8388608 | tf_op jit(solution)/shard_map/all_to_all | solution.py:34
  108.5 6.4 %copy.21 = bf16[64,8,16,256]{3,1,2,0:T(8,128)(2,1)} copy(bf16[64,8,16,256]{3,2,1,0:T(8,128)(2,1)} %bitcast.32) | data formatting | bytes 8388608
  114.9 201.6 %all-to-all-done.1 = bf16[16,256,1536]{2,1,0:T(8,128)(2,1)} async-done(((bf16[16,256,1536]{2,1,0:T(8,128)(2,1)}), bf16[16,256,1536]{2,1,0:T(8,128)(2,1)}, u32[]{:S(2)}, u32[]{:S(2)}) %all-to-all-start.1) | async-done | bytes 12582944 | tf_op jit(solution)/shard_map/all_to_all | solution.py:29
  316.6 12.1 %convolution_bitcast_fusion = f32[512,1536]{0,1:T(8,128)} fusion(bf16[4096,1536]{1,0:T(8,128)(2,1)} %bitcast.4, bf16[512,4096]{1,0:T(8,128)(2,1)} %bitcast.34), kind=kOutput, calls=%fused_computation | convolution fusion | flops 6442450944 | bytes 19922944 | tf_op jit(solution)/shard_map/dot_general | solution.py:36
  328.6 0.0 copy-start
  328.6 0.0 copy-start.1
  328.7 0.0 reduce-scatter.2.cloned.1.call-update
  328.7 0.7 copy-done
  329.4 18.0 %reduce-scatter.2.cloned.1.call-done = f32[256,1536]{0,1:T(8,128)} async-done(((f32[512,1536]{0,1:T(8,128)}), f32[256,1536]{0,1:T(8,128)}) %reduce-scatter.2.cloned.1.call-update) | async-done | bytes 1572880 | tf_op jit(solution)/shard_map/reduce_scatter | solution.py:37
  347.4 0.0 copy-done.1
  347.4 1.8 add_bitcast_fusion
  349.2 6.5 %copy.19 = f32[1,256,1536]{1,0,2:T(1,128)S(1)} copy(f32[1,256,1536]{1,2,0:T(8,128)S(1)} %add_bitcast_fusion) | data formatting | bytes 3145728 | tf_op jit(solution)/shard_map/broadcast_in_dim | solution.py:39
  355.7 25.3 %all_to_all.69 = f32[1,256,1536]{1,0,2:T(1,128)S(1)} all-to-all(f32[1,256,1536]{1,0,2:T(1,128)S(1)} %copy.19), channel_id=1, replica_groups=mesh['grp'=4,'chip'=16,'dc'=2] {'grp'}, dimensions={2} | all-to-all | bytes 3145728 | tf_op jit(solution)/shard_map/all_to_all | solution.py:39
  381.0 2.7 copy.20
  (1 shorter events, 0.0 us)
Async XLA Ops:
  6.5 17.7 %all-to-all-start = ((bf16[4,256,384]{2,1,0:T(8,128)(2,1)}), bf16[4,256,384]{2,1,0:T(8,128)(2,1)S(1)}, u32[]{:S(2)}, u32[]{:S(2)}) async-start(bf16[4,256,384]{2,1,0:T(8,128)(2,1)} %param.6), calls=%async_computation | async-start | bytes 1572864 | tf_op jit(solution)/shard_map/all_to_all | solution.py:21
  18.2 10.9 %copy-start.2 = (s32[4]{0:T(128)S(1)}, s32[4]{0:T(128)}, u32[]{:S(2)}) copy-start(s32[4]{0:T(128)} %param.9) | copy-start | bytes 52
  24.2 52.9 %all-to-all-start.2 = ((bf16[4,256,2048]{1,2,0:T(8,128)(2,1)}), bf16[4,256,2048]{1,2,0:T(8,128)(2,1)}, u32[]{:S(2)}, u32[]{:S(2)}) async-start(bf16[4,256,2048]{1,2,0:T(8,128)(2,1)} %copy.16), calls=%async_computation.2 | async-start | bytes 8388608 | tf_op jit(solution)/shard_map/all_to_all | solution.py:32
  93.4 223.1 %all-to-all-start.1 = ((bf16[16,256,1536]{2,1,0:T(8,128)(2,1)}), bf16[16,256,1536]{2,1,0:T(8,128)(2,1)}, u32[]{:S(2)}, u32[]{:S(2)}) async-start(bf16[16,256,1536]{2,1,0:T(8,128)(2,1)} %stack.2), calls=%async_computation.1 | async-start | bytes 25165824 | tf_op jit(solution)/shard_map/all_to_all | solution.py:29
  100.5 246.9 %reduce-scatter.2.cloned.1.call-start = ((), (), s32[]{:S(2)}) async-start(), calls=%async_computation.6 | async-start | bytes 4718592 | tf_op jit(solution)/shard_map/reduce_scatter | solution.py:37
  328.6 0.7 copy-start
  328.6 18.8 %copy-start.1 = (f32[1,256]{1,0:T(1,128)S(1)}, f32[1,256]{1,0:T(1,128)}, u32[]{:S(2)}) copy-start(f32[1,256]{1,0:T(1,128)} %param.7) | copy-start | bytes 3076
Sparse Core Ops, SparseCore 0:
  328.8 18.5 reduce-scatter.1
